TPU v7x, 32 devices: a whole 2x2x4 slice. The times are simulated.
32 devices in a mesh: groups: 2 (over y), dp: 16 (over z, x, core).
Axes of the slice: x: 2, y: 2, z: 4, core: 2. Of those that a mesh axis runs over, the one named last changes fastest.
Arguments:
- queries: bfloat16 [8192, 2048], P(('groups', 'dp')), parts along dimension 0, may hold values from -6 to 6
- grad_out: bfloat16 [8192, 2048], P(('groups', 'dp')), parts along dimension 0, may hold values from -60 to 60
- params: float32 [4096, 2048], P(('groups', 'dp')), parts along dimension 0, may hold values from -0.0625 to 0.0625
- first_moment: float32 [4096, 2048], P(('groups', 'dp')), parts along dimension 0, may hold values from -6 to 6
- second_moment: float32 [4096, 2048], P(('groups', 'dp')), parts along dimension 0, may hold values from 0.05 to 0.08
- key_params: float32 [4096, 2048], P(('groups', 'dp')), parts along dimension 0, may hold values from -0.0625 to 0.0625
- keys: bfloat16 [4096, 2048], P(('groups', 'dp')), parts along dimension 0, may hold values from -6 to 6
- perm: int32 [4096], P('groups'), parts along dimension 0, may hold values from 0 to 2047, as said below
- inv_perm: int32 [4096], P('groups'), parts along dimension 0, may hold values from 0 to 2047, as said below
- bn_gain: float32 [4096], P('groups'), parts along dimension 0, may hold values from 0.25 to 1.75
- bn_shift: float32 [4096], P('groups'), parts along dimension 0, may hold values from -3 to 3
- queue: bfloat16 [16, 2048, 2048], P('groups', 'dp'), parts along dimension 0, may hold values from -6 to 6
- slot: int32 [1], replicated, may hold values from 0 to 7
Outputs:
- new_params: float32 [4096, 2048], P(('groups', 'dp')), parts along dimension 0
- new_first: float32 [4096, 2048], P(('groups', 'dp')), parts along dimension 0
- new_second: float32 [4096, 2048], P(('groups', 'dp')), parts along dimension 0
- new_key: float32 [4096, 2048], P(('groups', 'dp')), parts along dimension 0
- new_queue: bfloat16 [16, 2048, 2048], P('groups', 'dp'), parts along dimension 0
There are 2 independent parts, one for each index of `groups`. A program takes and returns all parts, laid end to end along the dimension named above; an argument that names none is the same for every part. Nothing has to cross between parts.
Inputs may be any that keep to these rules, and one draw needn't show every extreme that they name: perm is a permutation of 0 to 2047; each aligned block of 128 of its entries holds exactly 8 values from every aligned block of 128 values. inv_perm[perm[i]] = i for every i.
All inputs are finite; a program needn't handle non-finite values.
Results may differ from a plain program's by a relative error of at most 0.0025.
Values may be sent and summed in bfloat16 or wider, within the bound.
No kernel may reach another device: no remote copies, remote signals or barrier semaphores. Data moves between devices by JAX's collectives and lax.ppermute only.
A program may use at most 128 MiB of HBM per device.

v0:
```python
import jax
import jax.numpy as jnp
from jax import lax
from jax.sharding import PartitionSpec as P

norm_epsilon = 1e-05
adam_epsilon = 1e-08
bias_first = 1.0 - 0.9**10
bias_second = 1.0 - 0.999**10


def route(mapping, position, block_rows, per_peer):
    members = mapping.shape[0] // block_rows
    layout = mapping.reshape(members, block_rows)
    owned = (layout // block_rows == position).astype(jnp.int32)
    ordinal = jnp.cumsum(owned, axis=1) - 1
    destination = jnp.arange(members, dtype=jnp.int32)[:, None] * per_peer + ordinal
    destination = jnp.where(owned == 1, destination, members * per_peer)
    offsets = jnp.where(owned == 1, layout - position * block_rows, 0)
    send_index = (
        jnp.zeros((members * per_peer + 1,), jnp.int32)
        .at[destination.reshape(-1)]
        .set(offsets.reshape(-1))[: members * per_peer]
    )
    own_block = lax.dynamic_slice_in_dim(mapping, position * block_rows, block_rows)
    anchor = own_block // block_rows
    indicator = (anchor[:, None] == jnp.arange(members, dtype=jnp.int32)[None, :]).astype(jnp.int32)
    arrival = jnp.sum((jnp.cumsum(indicator, axis=0) - 1) * indicator, axis=1)
    return (send_index, anchor * per_peer + arrival)


def grad_term(queries, grad_out):
    return lax.dot_general(
        queries, grad_out, (((0,), (0,)), ((), ())), preferred_element_type=jnp.float32
    )


def adamw(gradient, params, first_moment, second_moment, key_params):
    new_first = 0.9 * first_moment + 0.1 * gradient
    new_second = 0.999 * second_moment + 0.001 * gradient * gradient
    update = new_first / bias_first / (jnp.sqrt(new_second / bias_second) + adam_epsilon)
    new_params = params - 0.05 * (update + 0.1 * params)
    new_key = 0.99 * key_params + 0.01 * new_params
    return (new_params, new_first, new_second, new_key)


def batch_norm(codes, bn_gain, bn_shift):
    values = codes.astype(jnp.float32)
    center = jnp.mean(values, axis=0)
    spread = jnp.mean(jnp.square(values - center), axis=0)
    return jax.nn.relu(
        (values - center) * lax.rsqrt(spread + norm_epsilon) * bn_gain + bn_shift
    ).astype(jnp.bfloat16)


def per_device(
    queries,
    grad_out,
    params,
    first_moment,
    second_moment,
    key_params,
    keys,
    perm,
    inv_perm,
    bn_gain,
    bn_shift,
    queue,
    slot,
):
    position = lax.axis_index("dp")
    members = lax.axis_size("dp")
    block_rows = keys.shape[0]
    per_peer = block_rows // members
    scaling = 1.0 / jnp.sqrt(jnp.float32(queries.shape[0] * members))
    send_forward, receive_forward = route(perm, position, block_rows, per_peer)
    send_back, receive_back = route(inv_perm, position, block_rows, per_peer)
    moved = lax.all_to_all(
        jnp.take(keys, send_forward, axis=0), "dp", split_axis=0, concat_axis=0, tiled=True
    )
    encoded_rows = jnp.take(moved, receive_forward, axis=0)
    gradient = (
        lax.psum_scatter(grad_term(queries, grad_out), "dp", scatter_dimension=0, tiled=True)
        * scaling
    )
    new_params, new_first, new_second, new_key = adamw(
        gradient, params, first_moment, second_moment, key_params
    )
    codes = jnp.dot(
        encoded_rows,
        lax.all_gather(new_key.astype(jnp.bfloat16), "dp", axis=0, tiled=True),
        preferred_element_type=jnp.float32,
    )
    codes = codes.astype(jnp.bfloat16)
    normed = batch_norm(codes, bn_gain, bn_shift)
    returned = lax.all_to_all(
        jnp.take(normed, send_back, axis=0), "dp", split_axis=0, concat_axis=0, tiled=True
    )
    restored = jnp.take(returned, receive_back, axis=0)
    new_queue = lax.dynamic_update_slice(
        queue, restored[None], (slot[0], jnp.int32(0), jnp.int32(0))
    )
    return (new_params, new_first, new_second, new_key, new_queue)


def solution(mesh):
    in_specs = (
        P(("groups", "dp"), None),
        P(("groups", "dp"), None),
        P(("groups", "dp"), None),
        P(("groups", "dp"), None),
        P(("groups", "dp"), None),
        P(("groups", "dp"), None),
        P(("groups", "dp"), None),
        P("groups"),
        P("groups"),
        P("groups"),
        P("groups"),
        P("groups", "dp", None),
        P(),
    )
    out_specs = (
        P(("groups", "dp"), None),
        P(("groups", "dp"), None),
        P(("groups", "dp"), None),
        P(("groups", "dp"), None),
        P("groups", "dp", None),
    )
    return jax.shard_map(
        per_device, mesh=mesh, in_specs=in_specs, out_specs=out_specs, check_vma=False
    )
```

profile of v0, /device:TPU:0, one launch (start us, length us, event | category | flops | bytes accessed | tf_op | source)
XLA Modules:
  0.0 325.0 jit_solution(14405362757740360536)
XLA Ops:
  7.2 4.9 %copy.21 = bf16[8,128,2048]{2,1,0:T(8,128)(2,1)} copy(bf16[8,128,2048]{2,1,0:T(8,128)(2,1)} %param.26) | data formatting | bytes 8388608
  12.2 8.1 %fusion.29 = f32[2048,2048]{1,0:T(8,128)} fusion(bf16[256,2048]{1,0:T(8,128)(2,1)S(1)} %copy-done, bf16[256,2048]{1,0:T(8,128)(2,1)S(1)} %copy-done.2), kind=kOutput, calls=%fused_computation.102 | convolution fusion | flops 2147483648 | bytes 18874368 | tf_op jit(solution)/shard_map/dot_general | solution.py:33
  20.3 0.0 all-gather.2.cloned.1.call-start
  20.4 181.3 %reduce-scatter.2.cloned.1.call-done = f32[128,2048]{1,0:T(8,128)} async-done(((f32[2048,2048]{1,0:T(8,128)}), f32[128,2048]{1,0:T(8,128)}) %reduce-scatter.2.cloned.1.call-update) | async-done | bytes 1048592 | tf_op jit(solution)/shard_map/reduce_scatter | solution.py:83
  201.7 5.1 %fusion.27 = (bf16[128,2048]{1,0:T(8,128)(2,1)}, f32[128,2048]{1,0:T(8,128)}, f32[128,2048]{1,0:T(8,128)}, f32[128,2048]{1,0:T(8,128)}, f32[128,2048]{1,0:T(8,128)}) fusion(f32[128,2048]{1,0:T(8,128)S(1)} %copy-done.3, f32[128,2048]{1,0:T(8,128)} %param.17, f32[128,2048]{1,0:T(8,128)} %reduce-scatter.2.cloned.1.call-done, f32[128,2048]{1,0:T(8,128)} %param.18, ...), kind=kLoop, calls=%fused_computation.100 | loop fusion | flops 5242880 | bytes 9961472 | tf_op jit(solution)/shard_map/convert_element_type | solution.py:91
  206.9 0.3 reduce_window_sum.34
  207.2 0.3 reduce_window_sum.36
  207.4 0.1 subtract_select_fusion
  207.5 8.0 %scatter_custom_fusion = s32[129]{0:T(256)S(1)} fusion(s32[2048]{0:T(1024)S(1)} %get-tuple-element.25, s32[2048]{0:T(1024)S(1)} %get-tuple-element.26, s32[]{:T(128)} %constant.105.clone.1), kind=kCustom, calls=%fused_computation.97 | custom fusion | bytes 520 | tf_op jit(solution)/shard_map/scatter | solution.py:23
  215.6 0.9 gather_fusion
  216.5 1.0 select_bitcast_fusion.1
  217.5 3.7 %all-to-all-start = ((bf16[16,8,2048]{2,1,0:T(8,128)(2,1)}), bf16[16,8,2048]{2,1,0:T(8,128)(2,1)S(1)}, u32[]{:S(2)}, u32[]{:S(2)}) async-start(bf16[16,8,2048]{2,1,0:T(8,128)(2,1)} %select_bitcast_fusion.1), calls=%async_computation.1 | async-start | bytes 1048576 | tf_op jit(solution)/shard_map/all_to_all | solution.py:78
  221.2 0.1 and_select_fusion
  221.3 0.1 fusion.5
  221.4 0.2 reduce_window_sum.35
  221.6 8.0 %scatter_custom_fusion.1 = s32[129]{0:T(256)S(1)} fusion(s32[2048]{0:T(1024)S(1)} %get-tuple-element.20, s32[2048]{0:T(1024)S(1)} %get-tuple-element.19, s32[]{:T(128)} %constant.105.clone.1), kind=kCustom, calls=%fused_computation.95 | custom fusion | bytes 520 | tf_op jit(solution)/shard_map/scatter | solution.py:23
  229.6 0.2 select_reduce_fusion.1
  229.8 14.4 %all-to-all-done = bf16[16,8,2048]{2,1,0:T(8,128)(2,1)S(1)} async-done(((bf16[16,8,2048]{2,1,0:T(8,128)(2,1)}), bf16[16,8,2048]{2,1,0:T(8,128)(2,1)S(1)}, u32[]{:S(2)}, u32[]{:S(2)}) %all-to-all-start) | async-done | bytes 524320 | tf_op jit(solution)/shard_map/all_to_all | solution.py:78
  244.2 0.9 gather_fusion.1
  245.2 46.1 %all-gather.2.cloned.1.call-done = bf16[2048,2048]{1,0:T(8,128)(2,1)} async-done(((bf16[128,2048]{1,0:T(8,128)(2,1)}), bf16[2048,2048]{1,0:T(8,128)(2,1)}) %all-gather.2.cloned.1.call-update) | async-done | bytes 8388624 | tf_op jit(solution)/shard_map/all_gather | solution.py:91
  291.3 4.7 %fusion.28 = (f32[2048]{0:T(1024)S(1)}, f32[128,2048]{1,0:T(8,128)S(1)}) fusion(bf16[2048,2048]{1,0:T(8,128)(2,1)} %all-gather.2.cloned.1.call-done, bf16[128,2048]{1,0:T(8,128)(2,1)S(1)} %gather_fusion.1, pred[128]{0:T(512)(128)(4,1)S(1)} %get-tuple-element.10), kind=kOutput, calls=%fused_computation.101 | convolution fusion | flops 1074788352 | bytes 9969792 | tf_op jit(solution)/shard_map/dot_general | solution.py:89
  296.0 0.1 multiply_reduce_fusion
  296.2 0.2 maximum_convert_fusion
  296.4 0.9 gather_fusion.2
  297.4 0.9 select_bitcast_fusion
  298.3 3.6 %all-to-all-start.1 = ((bf16[16,8,2048]{2,1,0:T(8,128)(2,1)}), bf16[16,8,2048]{2,1,0:T(8,128)(2,1)S(1)}, u32[]{:S(2)}, u32[]{:S(2)}) async-start(bf16[16,8,2048]{2,1,0:T(8,128)(2,1)} %select_bitcast_fusion), calls=%async_computation.2 | async-start | bytes 1048576 | tf_op jit(solution)/shard_map/all_to_all | solution.py:96
  301.8 0.1 fusion.4
  301.9 0.2 reduce_window_sum.37
  302.8 0.2 select_reduce_fusion
  303.0 13.3 %all-to-all-done.1 = bf16[16,8,2048]{2,1,0:T(8,128)(2,1)S(1)} async-done(((bf16[16,8,2048]{2,1,0:T(8,128)(2,1)}), bf16[16,8,2048]{2,1,0:T(8,128)(2,1)S(1)}, u32[]{:S(2)}, u32[]{:S(2)}) %all-to-all-start.1) | async-done | bytes 524320 | tf_op jit(solution)/shard_map/all_to_all | solution.py:96
  316.3 0.9 gather_fusion.3
  317.2 1.0 bitcast_dynamic-update-slice_fusion
  (32 shorter events, 0.2 us)
Async XLA Ops:
  7.2 5.0 %copy-start = (bf16[256,2048]{1,0:T(8,128)(2,1)S(1)}, bf16[256,2048]{1,0:T(8,128)(2,1)}, u32[]{:S(2)}) copy-start(bf16[256,2048]{1,0:T(8,128)(2,1)} %param.15) | copy-start | bytes 3145732
  7.2 5.0 %copy-start.2 = (bf16[256,2048]{1,0:T(8,128)(2,1)S(1)}, bf16[256,2048]{1,0:T(8,128)(2,1)}, u32[]{:S(2)}) copy-start(bf16[256,2048]{1,0:T(8,128)(2,1)} %param.16) | copy-start | bytes 3145732
  7.2 194.5 %reduce-scatter.2.cloned.1.call-start = ((), (), s32[]{:S(2)}) async-start(), calls=%async_computation.3 | async-start | bytes 17825792 | tf_op jit(solution)/shard_map/reduce_scatter | solution.py:83
  20.3 181.4 %copy-start.3 = (f32[128,2048]{1,0:T(8,128)S(1)}, f32[128,2048]{1,0:T(8,128)}, u32[]{:S(2)}) copy-start(f32[128,2048]{1,0:T(8,128)} %param.20) | copy-start | bytes 3145732
  20.3 186.5 %copy-start.5 = (s32[2048]{0:T(1024)S(1)}, s32[2048]{0:T(1024)}, u32[]{:S(2)}) copy-start(s32[2048]{0:T(1024)} %param.22) | copy-start | bytes 24580
  20.3 186.8 %copy-start.4 = (s32[2048]{0:T(1024)S(1)}, s32[2048]{0:T(1024)}, u32[]{:S(2)}) copy-start(s32[2048]{0:T(1024)} %param.23) | copy-start | bytes 24580
  20.3 195.3 %copy-start.1 = (bf16[128,2048]{1,0:T(8,128)(2,1)S(1)}, bf16[128,2048]{1,0:T(8,128)(2,1)}, u32[]{:S(2)}) copy-start(bf16[128,2048]{1,0:T(8,128)(2,1)} %param.21) | copy-start | bytes 1572868
  20.3 270.9 %all-gather.2.cloned.1.call-start = ((), (), s32[]{:S(2)}) async-start(), calls=%async_computation.4 | async-start | bytes 8912896 | tf_op jit(solution)/shard_map/all_gather | solution.py:91
  217.5 26.7 %all-to-all-start = ((bf16[16,8,2048]{2,1,0:T(8,128)(2,1)}), bf16[16,8,2048]{2,1,0:T(8,128)(2,1)S(1)}, u32[]{:S(2)}, u32[]{:S(2)}) async-start(bf16[16,8,2048]{2,1,0:T(8,128)(2,1)} %select_bitcast_fusion.1), calls=%async_computation.1 | async-start | bytes 1048576 | tf_op jit(solution)/shard_map/all_to_all | solution.py:78
  291.3 4.9 %copy-start.6 = (f32[2048]{0:T(1024)S(1)}, f32[2048]{0:T(1024)}, u32[]{:S(2)}) copy-start(f32[2048]{0:T(1024)} %param.25) | copy-start | bytes 24580
  291.3 4.9 %copy-start.7 = (f32[2048]{0:T(1024)S(1)}, f32[2048]{0:T(1024)}, u32[]{:S(2)}) copy-start(f32[2048]{0:T(1024)} %param.24) | copy-start | bytes 24580
  298.3 18.0 %all-to-all-start.1 = ((bf16[16,8,2048]{2,1,0:T(8,128)(2,1)}), bf16[16,8,2048]{2,1,0:T(8,128)(2,1)S(1)}, u32[]{:S(2)}, u32[]{:S(2)}) async-start(bf16[16,8,2048]{2,1,0:T(8,128)(2,1)} %select_bitcast_fusion), calls=%async_computation.2 | async-start | bytes 1048576 | tf_op jit(solution)/shard_map/all_to_all | solution.py:96
Sparse Core Ops, SparseCore 0:
  20.4 181.2 reduce-scatter.1
  206.9 84.2 all-gather.1
where the time goes:
time: 325 us
  waiting for transfers between devices  255 us (78%)
  local copies, waits for them, and re-layouts  24.8 us (8%)
  between operations  14.9 us (5%)
  matrix products  12.8 us (4%)
  other arithmetic  9.96 us (3%)
  starting transfers between devices  7.34 us (2%)
    reduce_scatter x1, waiting for transfers between devices, per_device(): lax.psum_scatter(grad_term(queries, grad_out), 'dp', scatter_dimension=0,...  181 us
    all_gather x1, waiting for transfers between devices, per_device(): lax.all_gather(new_key.astype(jnp.bfloat16), 'dp', axis=0, tiled=True)  46.1 us
    scatter x2, local copies, waits for them, and re-layouts, route(): send_index = jnp.zeros((members * per_peer + 1,), jnp.int32).at[destinati...  16.1 us
    all_to_all x1, waiting for transfers between devices, per_device(): lax.all_to_all(jnp.take(keys, send_forward, axis=0), 'dp', split_axis=0,...  14.4 us
    all_to_all x1, waiting for transfers between devices, per_device(): lax.all_to_all(jnp.take(normed, send_back, axis=0), 'dp', split_axis=0, c...  13.3 us
    dot_general x1, matrix products, grad_term(): lax.dot_general(queries, grad_out, (((0,), (0,)), ((), ())), preferred_el...  8.1 us
  transfers between devices with their start and end apart: 4, of which 4 were waited for; matrix products, arithmetic and copies ran while one was open for 6% of the time, Pallas kernels for 0%

commit v1 on v0

--- a/solution.py
+++ b/solution.py
@@ -2,11 +2,28 @@
 import jax.numpy as jnp
 from jax import lax
 from jax.sharding import PartitionSpec as P
+from jax.lax import axis_index, axis_size, ppermute
 
 norm_epsilon = 1e-05
 adam_epsilon = 1e-08
 bias_first = 1.0 - 0.9**10
 bias_second = 1.0 - 0.999**10
+
+
+def _resolve_goods(u, peer_axis):
+    extent = axis_size(peer_axis)
+    parts_seen = tuple(((m, (m + 1) % extent) for m in range(extent)))
+    gallery = tuple(((m, (m - 1) % extent) for m in range(extent)))
+    frame_out, part_next = ([u], [u])
+    for _ in range(extent // 2):
+        f_next = ppermute(frame_out[-1], axis_name=peer_axis, perm=parts_seen)
+        frame_out.append(f_next)
+    for _ in range((extent - 1) // 2):
+        z1 = ppermute(part_next[-1], axis_name=peer_axis, perm=gallery)
+        part_next.append(z1)
+    all_rows = jnp.concatenate([*frame_out[::-1], *part_next[1:]], axis=0)
+    main = axis_index(peer_axis)
+    return jnp.roll(all_rows, (main - extent // 2) * u.shape[0], axis=0)
 
 
 def route(mapping, position, block_rows, per_peer):
@@ -88,7 +105,7 @@
     )
     codes = jnp.dot(
         encoded_rows,
-        lax.all_gather(new_key.astype(jnp.bfloat16), "dp", axis=0, tiled=True),
+        _resolve_goods(new_key.astype(jnp.bfloat16), "dp"),
         preferred_element_type=jnp.float32,
     )
     codes = codes.astype(jnp.bfloat16)

time: 325 us -> 372 us (1.14)
  starting transfers between devices: 7.34 us -> 51.8 us
  local copies, waits for them, and re-layouts: 24.8 us -> 49 us
  waiting for transfers between devices: 255 us -> 234 us
    all_gather x1 -> x0, waiting for transfers between devices: 46.1 us -> none  [per_device(): lax.all_gather(new_key.astype(jnp.bfloat16), 'dp', axis=0, tiled=True)]
    ppermute x0 -> x15, waiting for transfers between devices: none -> 39.3 us  [the longest x8 39.3 us: _resolve_goods(): f_next = ppermute(frame_out[-1], axis_name=peer_axis, perm=parts_seen)]
    ppermute x0 -> x15, starting transfers between devices: none -> 39.2 us  [the longest x7 28.5 us: _resolve_goods(): z1 = ppermute(part_next[-1], axis_name=peer_axis, perm=gallery)]
    unnamed x17 -> x56, local copies, waits for them, and re-layouts: 4.97 us -> 29.2 us
    all_to_all x1, waiting for transfers between devices: 14.4 us -> 0.01 us  [per_device(): lax.all_to_all(jnp.take(keys, send_forward, axis=0), 'dp', split_axis=0,...]
    all_to_all x1, starting transfers between devices: 3.69 us -> 9.02 us  [per_device(): lax.all_to_all(jnp.take(keys, send_forward, axis=0), 'dp', split_axis=0,...]
  transfers between devices with their start and end apart: 4 -> 18, of which waited for: 4 -> 7; matrix products, arithmetic and copies ran while one was open for 6% -> 9% of each run, Pallas kernels for 0% -> 0%
where the time goes in v1:
time: 372 us; the launch traced here: 371 us
  waiting for transfers between devices  234 us (63%)
  starting transfers between devices  51.8 us (14%)
  local copies, waits for them, and re-layouts  49 us (13%)
  between operations  15.3 us (4%)
  matrix products  10.8 us (3%)
  other arithmetic  9.7 us (3%)
    reduce_scatter x1, waiting for transfers between devices, per_device(): lax.psum_scatter(grad_term(queries, grad_out), 'dp', scatter_dimension=0,...  181 us
    ppermute x8, waiting for transfers between devices, _resolve_goods(): f_next = ppermute(frame_out[-1], axis_name=peer_axis, perm=parts_seen)  39.3 us
    unnamed x56, local copies, waits for them, and re-layouts  29.2 us
    ppermute x7, starting transfers between devices, _resolve_goods(): z1 = ppermute(part_next[-1], axis_name=peer_axis, perm=gallery)  28.5 us
    scatter x2, local copies, waits for them, and re-layouts, route(): send_index = jnp.zeros((members * per_peer + 1,), jnp.int32).at[destinati...  16.1 us
    all_to_all x1, waiting for transfers between devices, per_device(): lax.all_to_all(jnp.take(normed, send_back, axis=0), 'dp', split_axis=0, c...  13.3 us
    ppermute x8, starting transfers between devices, _resolve_goods(): f_next = ppermute(frame_out[-1], axis_name=peer_axis, perm=parts_seen)  10.7 us
    dot_general x1, matrix products, grad_term(): lax.dot_general(queries, grad_out, (((0,), (0,)), ((), ())), preferred_el...  9.44 us
  transfers between devices with their start and end apart: 18, of which 7 were waited for; matrix products, arithmetic and copies ran while one was open for 9% of the time, Pallas kernels for 0%

profile of v1, /device:TPU:0, one launch (start us, length us, event | category | flops | bytes accessed | tf_op | source)
XLA Modules:
  0.0 370.6 jit_solution(6219848816667013529)
XLA Ops:
  7.2 4.9 %copy.52 = bf16[8,128,2048]{2,1,0:T(8,128)(2,1)} copy(bf16[8,128,2048]{2,1,0:T(8,128)(2,1)} %param.26) | data formatting | bytes 8388608
  12.1 9.4 %fusion.37 = f32[2048,2048]{1,0:T(8,128)} fusion(bf16[256,2048]{1,0:T(8,128)(2,1)S(1)} %copy-done, bf16[256,2048]{1,0:T(8,128)(2,1)} %param.16), kind=kOutput, calls=%fused_computation.137 | convolution fusion | flops 2147483648 | bytes 18874368 | tf_op jit(solution)/shard_map/dot_general | solution.py:50
  21.6 181.4 %reduce-scatter.2.cloned.1.call-done = f32[128,2048]{1,0:T(8,128)} async-done(((f32[2048,2048]{1,0:T(8,128)}), f32[128,2048]{1,0:T(8,128)}) %reduce-scatter.2.cloned.1.call-update) | async-done | bytes 1048592 | tf_op jit(solution)/shard_map/reduce_scatter | solution.py:100
  203.0 4.9 %fusion.35 = (bf16[128,2048]{1,0:T(8,128)(2,1)S(1)}, f32[128,2048]{1,0:T(8,128)}, f32[128,2048]{1,0:T(8,128)}, f32[128,2048]{1,0:T(8,128)}, f32[128,2048]{1,0:T(8,128)}) fusion(f32[128,2048]{1,0:T(8,128)S(1)} %copy-done.7, f32[128,2048]{1,0:T(8,128)} %param.17, f32[128,2048]{1,0:T(8,128)} %reduce-scatter.2.cloned.1.call-done, f32[128,2048]{1,0:T(8,128)} %param.18, ...), kind=kLoop, calls=%fused_computation.135 | loop fusion | flops 5242880 | bytes 9961472 | tf_op jit(solution)/shard_map/convert_element_type | solution.py:108
  207.9 11.3 %collective-permute-done = bf16[128,2048]{1,0:T(8,128)(2,1)S(1)} collective-permute-done((bf16[128,2048]{1,0:T(8,128)(2,1)S(1)}, bf16[128,2048]{1,0:T(8,128)(2,1)S(1)}, u32[]{:S(2)}, u32[]{:S(2)}) %collective-permute-start) | collective-permute-done | bytes 524320 | tf_op jit(solution)/shard_map/ppermute | solution.py:19
  219.2 4.4 %collective-permute-start.8 = (bf16[128,2048]{1,0:T(8,128)(2,1)S(1)}, bf16[128,2048]{1,0:T(8,128)(2,1)S(1)}, u32[]{:S(2)}, u32[]{:S(2)}) collective-permute-start(bf16[128,2048]{1,0:T(8,128)(2,1)S(1)} %get-tuple-element.14), channel_id=1, source_target_pairs={{0,15},{1,0},{2,1},{3,2},{4,3},{5,4},{6,5},{7,6},{8,7},{9,8},{10,9... | collective-permute-start | bytes 1572872 | tf_op jit(solution)/shard_map/ppermute | solution.py:22
  223.7 7.0 %collective-permute-done.1 = bf16[128,2048]{1,0:T(8,128)(2,1)S(1)} collective-permute-done((bf16[128,2048]{1,0:T(8,128)(2,1)S(1)}, bf16[128,2048]{1,0:T(8,128)(2,1)S(1)}, u32[]{:S(2)}, u32[]{:S(2)}) %collective-permute-start.1) | collective-permute-done | bytes 524320 | tf_op jit(solution)/shard_map/ppermute | solution.py:19
  230.6 4.4 %collective-permute-start.9 = (bf16[128,2048]{1,0:T(8,128)(2,1)S(1)}, bf16[128,2048]{1,0:T(8,128)(2,1)S(1)}, u32[]{:S(2)}, u32[]{:S(2)}) collective-permute-start(bf16[128,2048]{1,0:T(8,128)(2,1)S(1)} %collective-permute-done.8), channel_id=1, source_target_pairs={{0,15},{1,0},{2,1},{3,2},{4,3},{5,4},{6,5},{7,6},{8,7},{9,8},{10,9... | collective-permute-start | bytes 1572872 | tf_op jit(solution)/shard_map/ppermute | solution.py:22
  235.1 7.1 %collective-permute-done.2 = bf16[128,2048]{1,0:T(8,128)(2,1)} collective-permute-done((bf16[128,2048]{1,0:T(8,128)(2,1)S(1)}, bf16[128,2048]{1,0:T(8,128)(2,1)}, u32[]{:S(2)}, u32[]{:S(2)}) %collective-permute-start.2) | collective-permute-done | bytes 524320 | tf_op jit(solution)/shard_map/ppermute | solution.py:19
  242.2 4.4 %collective-permute-start.10 = (bf16[128,2048]{1,0:T(8,128)(2,1)S(1)}, bf16[128,2048]{1,0:T(8,128)(2,1)}, u32[]{:S(2)}, u32[]{:S(2)}) collective-permute-start(bf16[128,2048]{1,0:T(8,128)(2,1)S(1)} %collective-permute-done.9), channel_id=1, source_target_pairs={{0,15},{1,0},{2,1},{3,2},{4,3},{5,4},{6,5},{7,6},{8,7},{9,8},{10,9... | collective-permute-start | bytes 1572872 | tf_op jit(solution)/shard_map/ppermute | solution.py:22
  246.6 7.3 %collective-permute-done.3 = bf16[128,2048]{1,0:T(8,128)(2,1)} collective-permute-done((bf16[128,2048]{1,0:T(8,128)(2,1)}, bf16[128,2048]{1,0:T(8,128)(2,1)}, u32[]{:S(2)}, u32[]{:S(2)}) %collective-permute-start.3) | collective-permute-done | bytes 524320 | tf_op jit(solution)/shard_map/ppermute | solution.py:19
  253.9 1.7 collective-permute-start.4
  256.2 2.8 collective-permute-start.11
  258.9 6.6 %collective-permute-done.4 = bf16[128,2048]{1,0:T(8,128)(2,1)} collective-permute-done((bf16[128,2048]{1,0:T(8,128)(2,1)}, bf16[128,2048]{1,0:T(8,128)(2,1)}, u32[]{:S(2)}, u32[]{:S(2)}) %collective-permute-start.4) | collective-permute-done | bytes 524320 | tf_op jit(solution)/shard_map/ppermute | solution.py:19
  265.6 4.5 %collective-permute-start.5 = (bf16[128,2048]{1,0:T(8,128)(2,1)}, bf16[128,2048]{1,0:T(8,128)(2,1)}, u32[]{:S(2)}, u32[]{:S(2)}) collective-permute-start(bf16[128,2048]{1,0:T(8,128)(2,1)} %collective-permute-done.4), channel_id=1, source_target_pairs={{0,1},{1,2},{2,3},{3,4},{4,5},{5,6},{6,7},{7,8},{8,9},{9,10},{10,1... | collective-permute-start | bytes 1572872 | tf_op jit(solution)/shard_map/ppermute | solution.py:19
  270.2 8.0 %scatter_custom_fusion = s32[129]{0:T(256)S(1)} fusion(s32[2048]{0:T(1024)S(1)} %get-tuple-element.27, s32[2048]{0:T(1024)S(1)} %get-tuple-element.28, s32[]{:T(128)} %constant.124.clone.1), kind=kCustom, calls=%fused_computation.131 | custom fusion | bytes 520 | tf_op jit(solution)/shard_map/scatter | solution.py:40
  279.3 2.5 collective-permute-start.6
  282.7 9.0 %all-to-all-start = ((bf16[16,8,2048]{2,1,0:T(8,128)(2,1)}), bf16[16,8,2048]{2,1,0:T(8,128)(2,1)S(1)}, u32[]{:S(2)}, u32[]{:S(2)}) async-start(bf16[16,8,2048]{2,1,0:T(8,128)(2,1)} %select_bitcast_fusion.1), calls=%async_computation.1 | async-start | bytes 1048576 | tf_op jit(solution)/shard_map/all_to_all | solution.py:95
  292.3 4.4 %collective-permute-start.13 = (bf16[128,2048]{1,0:T(8,128)(2,1)}, bf16[128,2048]{1,0:T(8,128)(2,1)}, u32[]{:S(2)}, u32[]{:S(2)}) collective-permute-start(bf16[128,2048]{1,0:T(8,128)(2,1)} %collective-permute-done.12), channel_id=1, source_target_pairs={{0,15},{1,0},{2,1},{3,2},{4,3},{5,4},{6,5},{7,6},{8,7},{9,8},{10,9... | collective-permute-start | bytes 1572872 | tf_op jit(solution)/shard_map/ppermute | solution.py:22
  296.7 1.9 collective-permute-start.7
  298.7 8.0 %scatter_custom_fusion.1 = s32[129]{0:T(256)S(1)} fusion(s32[2048]{0:T(1024)S(1)} %get-tuple-element.20, s32[2048]{0:T(1024)S(1)} %get-tuple-element.19, s32[]{:T(128)} %constant.124.clone.1), kind=kCustom, calls=%fused_computation.129 | custom fusion | bytes 520 | tf_op jit(solution)/shard_map/scatter | solution.py:40
  307.7 7.9 %collective-permute-start.14 = (bf16[128,2048]{1,0:T(8,128)(2,1)}, bf16[128,2048]{1,0:T(8,128)(2,1)S(1)}, u32[]{:S(2)}, u32[]{:S(2)}) collective-permute-start(bf16[128,2048]{1,0:T(8,128)(2,1)} %collective-permute-done.13), channel_id=1, source_target_pairs={{0,15},{1,0},{2,1},{3,2},{4,3},{5,4},{6,5},{7,6},{8,7},{9,8},{10,9... | collective-permute-start | bytes 1572872 | tf_op jit(solution)/shard_map/ppermute | solution.py:22
  316.7 1.1 constant_dynamic-update-slice_fusion.30
  317.8 1.1 constant_dynamic-update-slice_fusion.29
  318.9 1.1 constant_dynamic-update-slice_fusion.28
  320.0 1.1 constant_dynamic-update-slice_fusion.27
  321.1 1.1 constant_dynamic-update-slice_fusion.26
  324.5 1.1 constant_dynamic-update-slice_fusion.20
  335.8 1.2 constant_dynamic-update-slice_fusion.4
  340.3 1.3 fusion.36
  343.9 3.6 all-to-all-start.1
  348.6 13.3 %all-to-all-done.1 = bf16[16,8,2048]{2,1,0:T(8,128)(2,1)S(1)} async-done(((bf16[16,8,2048]{2,1,0:T(8,128)(2,1)}), bf16[16,8,2048]{2,1,0:T(8,128)(2,1)S(1)}, u32[]{:S(2)}, u32[]{:S(2)}) %all-to-all-start.1) | async-done | bytes 524320 | tf_op jit(solution)/shard_map/all_to_all | solution.py:113
  (99 shorter events, 25.3 us)
Async XLA Ops:
  7.2 4.9 %copy-start = (bf16[256,2048]{1,0:T(8,128)(2,1)S(1)}, bf16[256,2048]{1,0:T(8,128)(2,1)}, u32[]{:S(2)}) copy-start(bf16[256,2048]{1,0:T(8,128)(2,1)} %param.15) | copy-start | bytes 3145732
  7.2 195.8 %reduce-scatter.2.cloned.1.call-start = ((), (), s32[]{:S(2)}) async-start(), calls=%async_computation.3 | async-start | bytes 17825792 | tf_op jit(solution)/shard_map/reduce_scatter | solution.py:100
  12.1 190.9 %copy-start.7 = (f32[128,2048]{1,0:T(8,128)S(1)}, f32[128,2048]{1,0:T(8,128)}, u32[]{:S(2)}) copy-start(f32[128,2048]{1,0:T(8,128)} %param.20) | copy-start | bytes 3145732
  21.5 234.0 %copy-start.9 = (s32[2048]{0:T(1024)S(1)}, s32[2048]{0:T(1024)}, u32[]{:S(2)}) copy-start(s32[2048]{0:T(1024)} %param.22) | copy-start | bytes 24580
  21.5 234.3 %copy-start.8 = (s32[2048]{0:T(1024)S(1)}, s32[2048]{0:T(1024)}, u32[]{:S(2)}) copy-start(s32[2048]{0:T(1024)} %param.23) | copy-start | bytes 24580
  21.5 256.7 %copy-start.2 = (bf16[128,2048]{1,0:T(8,128)(2,1)S(1)}, bf16[128,2048]{1,0:T(8,128)(2,1)}, u32[]{:S(2)}) copy-start(bf16[128,2048]{1,0:T(8,128)(2,1)} %param.21) | copy-start | bytes 1572868
  207.9 11.3 %collective-permute-start = (bf16[128,2048]{1,0:T(8,128)(2,1)S(1)}, bf16[128,2048]{1,0:T(8,128)(2,1)S(1)}, u32[]{:S(2)}, u32[]{:S(2)}) collective-permute-start(bf16[128,2048]{1,0:T(8,128)(2,1)S(1)} %get-tuple-element.14), channel_id=1, source_target_pairs={{0,1},{1,2},{2,3},{3,4},{4,5},{5,6},{6,7},{7,8},{8,9},{9,10},{10,1... | collective-permute-start | bytes 1572872 | tf_op jit(solution)/shard_map/ppermute | solution.py:19
  219.2 11.4 %collective-permute-start.1 = (bf16[128,2048]{1,0:T(8,128)(2,1)S(1)}, bf16[128,2048]{1,0:T(8,128)(2,1)S(1)}, u32[]{:S(2)}, u32[]{:S(2)}) collective-permute-start(bf16[128,2048]{1,0:T(8,128)(2,1)S(1)} %collective-permute-done), channel_id=1, source_target_pairs={{0,1},{1,2},{2,3},{3,4},{4,5},{5,6},{6,7},{7,8},{8,9},{9,10},{10,1... | collective-permute-start | bytes 1572872 | tf_op jit(solution)/shard_map/ppermute | solution.py:19
  219.2 11.4 %collective-permute-start.8 = (bf16[128,2048]{1,0:T(8,128)(2,1)S(1)}, bf16[128,2048]{1,0:T(8,128)(2,1)S(1)}, u32[]{:S(2)}, u32[]{:S(2)}) collective-permute-start(bf16[128,2048]{1,0:T(8,128)(2,1)S(1)} %get-tuple-element.14), channel_id=1, source_target_pairs={{0,15},{1,0},{2,1},{3,2},{4,3},{5,4},{6,5},{7,6},{8,7},{9,8},{10,9... | collective-permute-start | bytes 1572872 | tf_op jit(solution)/shard_map/ppermute | solution.py:22
  230.6 47.6 %copy-start.3 = (bf16[128,2048]{1,0:T(8,128)(2,1)}, bf16[128,2048]{1,0:T(8,128)(2,1)S(1)}, u32[]{:S(2)}) copy-start(bf16[128,2048]{1,0:T(8,128)(2,1)S(1)} %collective-permute-done.1) | copy-start | bytes 1572868
  230.6 11.5 %collective-permute-start.2 = (bf16[128,2048]{1,0:T(8,128)(2,1)S(1)}, bf16[128,2048]{1,0:T(8,128)(2,1)}, u32[]{:S(2)}, u32[]{:S(2)}) collective-permute-start(bf16[128,2048]{1,0:T(8,128)(2,1)S(1)} %collective-permute-done.1), channel_id=1, source_target_pairs={{0,1},{1,2},{2,3},{3,4},{4,5},{5,6},{6,7},{7,8},{8,9},{9,10},{10,1... | collective-permute-start | bytes 1572872 | tf_op jit(solution)/shard_map/ppermute | solution.py:19
  230.6 11.5 %collective-permute-start.9 = (bf16[128,2048]{1,0:T(8,128)(2,1)S(1)}, bf16[128,2048]{1,0:T(8,128)(2,1)S(1)}, u32[]{:S(2)}, u32[]{:S(2)}) collective-permute-start(bf16[128,2048]{1,0:T(8,128)(2,1)S(1)} %collective-permute-done.8), channel_id=1, source_target_pairs={{0,15},{1,0},{2,1},{3,2},{4,3},{5,4},{6,5},{7,6},{8,7},{9,8},{10,9... | collective-permute-start | bytes 1572872 | tf_op jit(solution)/shard_map/ppermute | solution.py:22
  242.1 11.7 %collective-permute-start.3 = (bf16[128,2048]{1,0:T(8,128)(2,1)}, bf16[128,2048]{1,0:T(8,128)(2,1)}, u32[]{:S(2)}, u32[]{:S(2)}) collective-permute-start(bf16[128,2048]{1,0:T(8,128)(2,1)} %collective-permute-done.2), channel_id=1, source_target_pairs={{0,1},{1,2},{2,3},{3,4},{4,5},{5,6},{6,7},{7,8},{8,9},{9,10},{10,1... | collective-permute-start | bytes 1572872 | tf_op jit(solution)/shard_map/ppermute | solution.py:19
  242.1 64.6 %copy-start.5 = (bf16[128,2048]{1,0:T(8,128)(2,1)}, bf16[128,2048]{1,0:T(8,128)(2,1)S(1)}, u32[]{:S(2)}) copy-start(bf16[128,2048]{1,0:T(8,128)(2,1)S(1)} %collective-permute-done.9) | copy-start | bytes 1572868
  242.2 14.0 %collective-permute-start.10 = (bf16[128,2048]{1,0:T(8,128)(2,1)S(1)}, bf16[128,2048]{1,0:T(8,128)(2,1)}, u32[]{:S(2)}, u32[]{:S(2)}) collective-permute-start(bf16[128,2048]{1,0:T(8,128)(2,1)S(1)} %collective-permute-done.9), channel_id=1, source_target_pairs={{0,15},{1,0},{2,1},{3,2},{4,3},{5,4},{6,5},{7,6},{8,7},{9,8},{10,9... | collective-permute-start | bytes 1572872 | tf_op jit(solution)/shard_map/ppermute | solution.py:22
  253.9 11.7 %collective-permute-start.4 = (bf16[128,2048]{1,0:T(8,128)(2,1)}, bf16[128,2048]{1,0:T(8,128)(2,1)}, u32[]{:S(2)}, u32[]{:S(2)}) collective-permute-start(bf16[128,2048]{1,0:T(8,128)(2,1)} %collective-permute-done.3), channel_id=1, source_target_pairs={{0,1},{1,2},{2,3},{3,4},{4,5},{5,6},{6,7},{7,8},{8,9},{9,10},{10,1... | collective-permute-start | bytes 1572872 | tf_op jit(solution)/shard_map/ppermute | solution.py:19
  256.2 23.0 %collective-permute-start.11 = (bf16[128,2048]{1,0:T(8,128)(2,1)}, bf16[128,2048]{1,0:T(8,128)(2,1)}, u32[]{:S(2)}, u32[]{:S(2)}) collective-permute-start(bf16[128,2048]{1,0:T(8,128)(2,1)} %collective-permute-done.10), channel_id=1, source_target_pairs={{0,15},{1,0},{2,1},{3,2},{4,3},{5,4},{6,5},{7,6},{8,7},{9,8},{10,9... | collective-permute-start | bytes 1572872 | tf_op jit(solution)/shard_map/ppermute | solution.py:22
  265.6 13.7 %collective-permute-start.5 = (bf16[128,2048]{1,0:T(8,128)(2,1)}, bf16[128,2048]{1,0:T(8,128)(2,1)}, u32[]{:S(2)}, u32[]{:S(2)}) collective-permute-start(bf16[128,2048]{1,0:T(8,128)(2,1)} %collective-permute-done.4), channel_id=1, source_target_pairs={{0,1},{1,2},{2,3},{3,4},{4,5},{5,6},{6,7},{7,8},{8,9},{9,10},{10,1... | collective-permute-start | bytes 1572872 | tf_op jit(solution)/shard_map/ppermute | solution.py:19
  279.2 13.1 %collective-permute-start.12 = (bf16[128,2048]{1,0:T(8,128)(2,1)}, bf16[128,2048]{1,0:T(8,128)(2,1)}, u32[]{:S(2)}, u32[]{:S(2)}) collective-permute-start(bf16[128,2048]{1,0:T(8,128)(2,1)} %collective-permute-done.11), channel_id=1, source_target_pairs={{0,15},{1,0},{2,1},{3,2},{4,3},{5,4},{6,5},{7,6},{8,7},{9,8},{10,9... | collective-permute-start | bytes 1572872 | tf_op jit(solution)/shard_map/ppermute | solution.py:22
  279.3 17.4 %collective-permute-start.6 = (bf16[128,2048]{1,0:T(8,128)(2,1)}, bf16[128,2048]{1,0:T(8,128)(2,1)}, u32[]{:S(2)}, u32[]{:S(2)}) collective-permute-start(bf16[128,2048]{1,0:T(8,128)(2,1)} %collective-permute-done.5), channel_id=1, source_target_pairs={{0,1},{1,2},{2,3},{3,4},{4,5},{5,6},{6,7},{7,8},{8,9},{9,10},{10,1... | collective-permute-start | bytes 1572872 | tf_op jit(solution)/shard_map/ppermute | solution.py:19
  282.7 52.8 %copy-start.4 = (bf16[128,2048]{1,0:T(8,128)(2,1)S(1)}, bf16[128,2048]{1,0:T(8,128)(2,1)}, u32[]{:S(2)}) copy-start(bf16[128,2048]{1,0:T(8,128)(2,1)} %copy-done.3) | copy-start | bytes 1572868
  282.7 24.0 %all-to-all-start = ((bf16[16,8,2048]{2,1,0:T(8,128)(2,1)}), bf16[16,8,2048]{2,1,0:T(8,128)(2,1)S(1)}, u32[]{:S(2)}, u32[]{:S(2)}) async-start(bf16[16,8,2048]{2,1,0:T(8,128)(2,1)} %select_bitcast_fusion.1), calls=%async_computation.1 | async-start | bytes 1048576 | tf_op jit(solution)/shard_map/all_to_all | solution.py:95
  292.3 15.4 %collective-permute-start.13 = (bf16[128,2048]{1,0:T(8,128)(2,1)}, bf16[128,2048]{1,0:T(8,128)(2,1)}, u32[]{:S(2)}, u32[]{:S(2)}) collective-permute-start(bf16[128,2048]{1,0:T(8,128)(2,1)} %collective-permute-done.12), channel_id=1, source_target_pairs={{0,15},{1,0},{2,1},{3,2},{4,3},{5,4},{6,5},{7,6},{8,7},{9,8},{10,9... | collective-permute-start | bytes 1572872 | tf_op jit(solution)/shard_map/ppermute | solution.py:22
  296.7 18.9 %collective-permute-start.7 = (bf16[128,2048]{1,0:T(8,128)(2,1)}, bf16[128,2048]{1,0:T(8,128)(2,1)}, u32[]{:S(2)}, u32[]{:S(2)}) collective-permute-start(bf16[128,2048]{1,0:T(8,128)(2,1)} %collective-permute-done.6), channel_id=1, source_target_pairs={{0,1},{1,2},{2,3},{3,4},{4,5},{5,6},{6,7},{7,8},{8,9},{9,10},{10,1... | collective-permute-start | bytes 1572872 | tf_op jit(solution)/shard_map/ppermute | solution.py:19
  307.7 28.0 %copy-start.6 = (bf16[128,2048]{1,0:T(8,128)(2,1)S(1)}, bf16[128,2048]{1,0:T(8,128)(2,1)}, u32[]{:S(2)}) copy-start(bf16[128,2048]{1,0:T(8,128)(2,1)} %copy-done.5) | copy-start | bytes 1572868
  307.7 21.2 %collective-permute-start.14 = (bf16[128,2048]{1,0:T(8,128)(2,1)}, bf16[128,2048]{1,0:T(8,128)(2,1)S(1)}, u32[]{:S(2)}, u32[]{:S(2)}) collective-permute-start(bf16[128,2048]{1,0:T(8,128)(2,1)} %collective-permute-done.13), channel_id=1, source_target_pairs={{0,15},{1,0},{2,1},{3,2},{4,3},{5,4},{6,5},{7,6},{8,7},{9,8},{10,9... | collective-permute-start | bytes 1572872 | tf_op jit(solution)/shard_map/ppermute | solution.py:22
  324.5 17.3 %copy-start.10 = (f32[2048]{0:T(1024)S(1)}, f32[2048]{0:T(1024)}, u32[]{:S(2)}) copy-start(f32[2048]{0:T(1024)} %param.25) | copy-start | bytes 24580
  324.5 17.3 %copy-start.11 = (f32[2048]{0:T(1024)S(1)}, f32[2048]{0:T(1024)}, u32[]{:S(2)}) copy-start(f32[2048]{0:T(1024)} %param.24) | copy-start | bytes 24580
  335.6 28.2 %copy-start.1 = (bf16[256,2048]{1,0:T(8,128)(2,1)S(1)}, bf16[256,2048]{1,0:T(8,128)(2,1)}, u32[]{:S(2)}) copy-start(bf16[256,2048]{1,0:T(8,128)(2,1)} %param.15) | copy-start | bytes 3145732
  343.9 18.0 %all-to-all-start.1 = ((bf16[16,8,2048]{2,1,0:T(8,128)(2,1)}), bf16[16,8,2048]{2,1,0:T(8,128)(2,1)S(1)}, u32[]{:S(2)}, u32[]{:S(2)}) async-start(bf16[16,8,2048]{2,1,0:T(8,128)(2,1)} %select_bitcast_fusion), calls=%async_computation.2 | async-start | bytes 1048576 | tf_op jit(solution)/shard_map/all_to_all | solution.py:113
Sparse Core Ops, SparseCore 0:
  21.7 181.2 reduce-scatter.1
